TPU v7x, 32 devices: a whole 2x2x4 slice. The times are simulated.
32 devices in a mesh: row: 8 (over y, x, core), col: 4 (over z).
Axes of the slice: x: 2, y: 2, z: 4, core: 2. Of those that a mesh axis runs over, the one named last changes fastest.
Arguments:
- pair: bfloat16 [256, 256, 128], P('row', 'col'), may hold values from -6 to 6
- mask: int32 [256], replicated, may hold values 0 or 1
- w_agate: bfloat16 [128, 128], replicated, may hold values from -0.5 to 0.5
- w_aproj: bfloat16 [128, 128], replicated, may hold values from -0.5 to 0.5
- w_bgate: bfloat16 [128, 128], replicated, may hold values from -0.5 to 0.5
- w_bproj: bfloat16 [128, 128], replicated, may hold values from -0.5 to 0.5
- w_gate: bfloat16 [128, 128], replicated, may hold values from -0.5 to 0.5
- w_out: bfloat16 [128, 128], replicated, may hold values from -0.5 to 0.5
- w_up: bfloat16 [128, 512], replicated, may hold values from -0.5 to 0.5
- w_down: bfloat16 [512, 128], replicated, may hold values from -0.25 to 0.25
Outputs:
- updated: bfloat16 [256, 256, 128], P('row', 'col')
All inputs are finite; a program needn't handle non-finite values.
Results may differ from a plain program's by a relative error of at most 0.0059.
Values may be sent and summed in bfloat16 or wider, within the bound.
No kernel may reach another device: no remote copies, remote signals or barrier semaphores. Data moves between devices by JAX's collectives and lax.ppermute only.
A program may use at most 64 MiB of HBM per device.

v0:
```python
import jax
import jax.numpy as jnp
from jax import lax
from jax.sharding import PartitionSpec as P


def layer_norm(values):
    center = values - jnp.mean(values, axis=-1, keepdims=True)
    spread = jnp.mean(center * center, axis=-1, keepdims=True)
    return center * lax.rsqrt(spread + 1e-05)


def body(pair, mask, w_agate, w_aproj, w_bgate, w_bproj, w_gate, w_out, w_up, w_down):
    rows, cols, width = pair.shape
    present = mask.astype(jnp.float32)
    row_start = lax.axis_index("row") * rows
    col_start = lax.axis_index("col") * cols
    row_mask = lax.dynamic_slice_in_dim(present, row_start, rows, 0)
    col_mask = lax.dynamic_slice_in_dim(present, col_start, cols, 0)
    pair_mask = (row_mask[:, None] * col_mask[None, :]).reshape(rows * cols, 1)
    pair_flat = pair.astype(jnp.float32).reshape(rows * cols, width)
    normed = layer_norm(pair_flat).astype(jnp.bfloat16)
    gate = jax.nn.sigmoid(jnp.dot(normed, w_gate, preferred_element_type=jnp.float32))
    left = (
        jax.nn.sigmoid(jnp.dot(normed, w_agate, preferred_element_type=jnp.float32))
        * jnp.dot(normed, w_aproj, preferred_element_type=jnp.float32)
        * pair_mask
    )
    right = (
        jax.nn.sigmoid(jnp.dot(normed, w_bgate, preferred_element_type=jnp.float32))
        * jnp.dot(normed, w_bproj, preferred_element_type=jnp.float32)
        * pair_mask
    )
    left_major = jnp.transpose(left.astype(jnp.bfloat16).reshape(rows, cols, -1), (2, 0, 1))
    right_major = jnp.transpose(right.astype(jnp.bfloat16).reshape(rows, cols, -1), (2, 0, 1))
    left_spread, right_spread = (
        lax.all_to_all(
            lax.all_to_all(left_major, "row", split_axis=0, concat_axis=1, tiled=True),
            "col",
            split_axis=1,
            concat_axis=2,
            tiled=True,
        ),
        lax.all_to_all(
            lax.all_to_all(right_major, "row", split_axis=0, concat_axis=1, tiled=True),
            "col",
            split_axis=1,
            concat_axis=2,
            tiled=True,
        ),
    )
    mixed = jnp.einsum(
        "cik,cjk->cij",
        lax.all_gather(left_spread, "col", axis=1, tiled=True),
        right_spread,
        preferred_element_type=jnp.float32,
    ).astype(jnp.bfloat16)
    mixed = lax.all_to_all(mixed, "row", split_axis=1, concat_axis=0, tiled=True)
    mixed_rows = jnp.transpose(mixed, (1, 2, 0)).astype(jnp.float32).reshape(rows * cols, -1)
    mixed_normed = layer_norm(mixed_rows).astype(jnp.bfloat16)
    middle = pair_flat + gate * jnp.dot(mixed_normed, w_out, preferred_element_type=jnp.float32)
    trans_in = layer_norm(middle).astype(jnp.bfloat16)
    trans_hidden = jax.nn.relu(jnp.dot(trans_in, w_up, preferred_element_type=jnp.float32)).astype(
        jnp.bfloat16
    )
    result = middle + jnp.dot(trans_hidden, w_down, preferred_element_type=jnp.float32)
    return result.astype(jnp.bfloat16).reshape(rows, cols, width)


def solution(mesh):
    placed = (P("row", "col", None), P(), P(), P(), P(), P(), P(), P(), P(), P())
    return jax.shard_map(
        body, mesh=mesh, in_specs=placed, out_specs=P("row", "col", None), check_vma=False
    )
```

profile of v0, /device:TPU:0, one launch (start us, length us, event | category | flops | bytes accessed | tf_op | source)
XLA Modules:
  0.0 144.5 jit_solution(13755586689063979857)
XLA Ops:
  6.5 1.4 convert_reduce_fusion
  8.0 1.7 %multiply_reduce_fusion.2 = f32[32,64]{1,0:T(8,128)S(1)} fusion(bf16[32,64,128]{2,1,0:T(8,128)(2,1)} %param.10, f32[32,64]{1,0:T(8,128)S(1)} %broadcast_multiply_fusion.2), kind=kLoop, calls=%fused_computation.36 | loop fusion | flops 1046528 | bytes 540672 | tf_op jit(solution)/shard_map/reduce_sum | solution.py:9
  10.8 1.6 %fusion.18 = bf16[2048,128]{1,0:T(8,128)(2,1)S(1)} fusion(bf16[32,64,128]{2,1,0:T(8,128)(2,1)} %param.10, f32[2048]{0:T(1024)S(1)} %rsqrt.31, f32[2048]{0:T(1024)S(1)} %div.32), kind=kLoop, calls=%fused_computation.33 | loop fusion | flops 1048576 | bytes 1064960 | tf_op jit(solution)/shard_map/convert_element_type | solution.py:22
  13.6 1.6 %copy.22 = bf16[32,64,128]{1,0,2:T(8,128)(2,1)S(1)} copy(bf16[32,64,128]{2,1,0:T(8,128)(2,1)S(1)} %bitcast.89) | data formatting | bytes 1048576 | tf_op jit(solution)/shard_map/reshape | solution.py:34
  15.9 14.7 %all_to_all.81 = bf16[8,2,16384]{2,1,0:T(2,128)(2,1)S(1)} all-to-all(bf16[8,2,16384]{2,1,0:T(2,128)(2,1)S(1)} %reshape.119), channel_id=1, replica_groups=mesh['row'=8,'col'=4] {'row'}, dimensions={0} | all-to-all | bytes 1048576 | tf_op jit(solution)/shard_map/all_to_all | solution.py:38
  32.1 0.9 reshape.121
  33.0 18.5 %all_to_all.82 = bf16[4,2,32768]{2,1,0:T(2,128)(2,1)S(1)} all-to-all(bf16[4,2,32768]{2,1,0:T(2,128)(2,1)S(1)} %reshape.121), channel_id=1, replica_groups=mesh['row'=8,'col'=4] {'col'}, dimensions={0} | all-to-all | bytes 1048576 | tf_op jit(solution)/shard_map/all_to_all | solution.py:37
  52.2 0.8 copy.45
  53.0 1.5 %all_to_all.66 = bf16[16,64,256]{2,1,0:T(8,128)(2,1)} reshape(bf16[16,64,4,64]{3,2,1,0:T(4,128)(2,1)S(1)} %bitcast.81) | data formatting | bytes 1048576 | tf_op jit(solution)/shard_map/all_to_all | solution.py:37
  55.7 1.6 %copy.27 = bf16[32,64,128]{1,0,2:T(8,128)(2,1)S(1)} copy(bf16[32,64,128]{2,1,0:T(8,128)(2,1)S(1)} %bitcast.88) | data formatting | bytes 1048576 | tf_op jit(solution)/shard_map/reshape | solution.py:35
  58.0 12.2 %all_to_all.83 = bf16[8,2,16384]{2,1,0:T(2,128)(2,1)S(1)} all-to-all(bf16[8,2,16384]{2,1,0:T(2,128)(2,1)S(1)} %reshape.123), channel_id=1, replica_groups=mesh['row'=8,'col'=4] {'row'}, dimensions={0} | all-to-all | bytes 1048576 | tf_op jit(solution)/shard_map/all_to_all | solution.py:45
  71.6 0.9 reshape.125
  72.5 31.4 %all_to_all.84 = bf16[4,2,32768]{2,1,0:T(2,128)(2,1)S(1)} all-to-all(bf16[4,2,32768]{2,1,0:T(2,128)(2,1)S(1)} %reshape.125), channel_id=1, replica_groups=mesh['row'=8,'col'=4] {'col'}, dimensions={0} | all-to-all | bytes 1048576 | tf_op jit(solution)/shard_map/all_to_all | solution.py:44
  104.6 0.8 copy.44
  106.1 3.6 %all-gather.2.cloned.1.call-done = bf16[16,256,256]{2,1,0:T(8,128)(2,1)} async-done(((bf16[16,64,256]{2,1,0:T(8,128)(2,1)}), bf16[16,256,256]{2,1,0:T(8,128)(2,1)}) %all-gather.2.cloned.1.call-update) | async-done | bytes 2097168 | tf_op jit(solution)/shard_map/all_gather | solution.py:54
  109.7 2.3 %convolution_convert_fusion = bf16[16,256,64]{1,2,0:T(8,128)(2,1)S(1)} fusion(bf16[16,256,256]{2,1,0:T(8,128)(2,1)} %all-gather.2.cloned.1.call-done, bf16[16,64,256]{2,1,0:T(8,128)(2,1)S(1)} %all_to_all.74), kind=kOutput, calls=%fused_computation.25 | convolution fusion | flops 134479872 | bytes 3145728 | tf_op jit(solution)/shard_map/cik,cjk->cij/dot_general | solution.py:52
  112.0 1.0 copy.32
  113.0 1.5 %reshape.127 = bf16[8,2,16384]{2,1,0:T(2,128)(2,1)} reshape(bf16[256,16,64]{2,1,0:T(8,128)(2,1)S(1)} %bitcast.76) | data formatting | bytes 1048576
  114.5 3.7 %all-to-all-start.4 = ((bf16[8,2,16384]{2,1,0:T(2,128)(2,1)}), bf16[8,2,16384]{2,1,0:T(2,128)(2,1)S(1)}, u32[]{:S(2)}, u32[]{:S(2)}) async-start(bf16[8,2,16384]{2,1,0:T(2,128)(2,1)} %reshape.127), calls=%async_computation.4 | async-start | bytes 1048576 | tf_op jit(solution)/shard_map/all_to_all | solution.py:58
  118.2 1.4 fusion.11
  119.6 8.3 %all-to-all-done.4 = bf16[8,2,16384]{2,1,0:T(2,128)(2,1)S(1)} async-done(((bf16[8,2,16384]{2,1,0:T(2,128)(2,1)}), bf16[8,2,16384]{2,1,0:T(2,128)(2,1)S(1)}, u32[]{:S(2)}, u32[]{:S(2)}) %all-to-all-start.4) | async-done | bytes 524320 | tf_op jit(solution)/shard_map/all_to_all | solution.py:58
  130.1 2.3 %copy.35 = f32[32,64,128]{2,1,0:T(8,128)} copy(f32[32,64,128]{1,0,2:T(8,128)S(1)} %bitcast.71) | data formatting | bytes 2097152 | tf_op jit(solution)/shard_map/convert_element_type | solution.py:59
  132.4 1.9 %fusion.16 = bf16[2048,128]{1,0:T(8,128)(2,1)S(1)} fusion(f32[32,64,128]{2,1,0:T(8,128)} %copy.35, f32[2048]{0:T(1024)S(1)} %rsqrt.33, f32[2048]{0:T(1024)S(1)} %div.38), kind=kLoop, calls=%fused_computation.28 | loop fusion | flops 786432 | bytes 1589248 | tf_op jit(solution)/shard_map/convert_element_type | solution.py:60
  135.5 2.1 %fusion.14 = bf16[2048,128]{1,0:T(8,128)(2,1)} fusion(f32[2048,128]{1,0:T(8,128)S(1)} %get-tuple-element.6, bf16[512,128]{1,0:T(8,128)(2,1)S(1)} %copy-done, bf16[128,512]{1,0:T(8,128)(2,1)S(1)} %copy-done.6, f32[2048]{0:T(1024)S(1)} %add_rsqrt_fusion.2, f32[2048]{0:T(1024)S(1)} %broadcast_multiply_fusion.3), kind=kOutput, calls=%fused_computation.22 | convolution fusion | flops 540278784 | bytes 1851392 | tf_op jit(solution)/shard_map/dot_general | solution.py:66
  (60 shorter events, 13.0 us)
Async XLA Ops:
  6.5 129.0 %copy-start = (bf16[512,128]{1,0:T(8,128)(2,1)S(1)}, bf16[512,128]{1,0:T(8,128)(2,1)}, u32[]{:S(2)}) copy-start(bf16[512,128]{1,0:T(8,128)(2,1)} %param.19) | copy-start | bytes 393220
  6.5 5.9 %copy-start.7 = (bf16[128,128]{1,0:T(8,128)(2,1)S(1)}, bf16[128,128]{1,0:T(8,128)(2,1)}, u32[]{:S(2)}) copy-start(bf16[128,128]{1,0:T(8,128)(2,1)} %param.12) | copy-start | bytes 98308
  6.5 103.1 %all-gather.2.cloned.1.call-start = ((), (), s32[]{:S(2)}) async-start(), calls=%async_computation.5 | async-start | bytes 2621440 | tf_op jit(solution)/shard_map/all_gather | solution.py:54
  12.5 0.8 copy-start.3
  52.2 2.3 %copy-start.8 = (bf16[128,128]{1,0:T(8,128)(2,1)S(1)}, bf16[128,128]{1,0:T(8,128)(2,1)}, u32[]{:S(2)}) copy-start(bf16[128,128]{1,0:T(8,128)(2,1)} %param.14) | copy-start | bytes 98308
  54.5 0.8 copy-start.4
  112.0 6.2 %copy-start.9 = (bf16[128,128]{1,0:T(8,128)(2,1)S(1)}, bf16[128,128]{1,0:T(8,128)(2,1)}, u32[]{:S(2)}) copy-start(bf16[128,128]{1,0:T(8,128)(2,1)} %param.16) | copy-start | bytes 98308
  114.5 13.4 %all-to-all-start.4 = ((bf16[8,2,16384]{2,1,0:T(2,128)(2,1)}), bf16[8,2,16384]{2,1,0:T(2,128)(2,1)S(1)}, u32[]{:S(2)}, u32[]{:S(2)}) async-start(bf16[8,2,16384]{2,1,0:T(2,128)(2,1)} %reshape.127), calls=%async_computation.4 | async-start | bytes 1048576 | tf_op jit(solution)/shard_map/all_to_all | solution.py:58
  130.0 4.3 %copy-start.1 = (bf16[32,64,128]{2,1,0:T(8,128)(2,1)S(1)}, bf16[32,64,128]{2,1,0:T(8,128)(2,1)}, u32[]{:S(2)}) copy-start(bf16[32,64,128]{2,1,0:T(8,128)(2,1)} %param.10) | copy-start | bytes 1572868
  130.1 4.3 %copy-start.5 = (bf16[128,128]{1,0:T(8,128)(2,1)S(1)}, bf16[128,128]{1,0:T(8,128)(2,1)}, u32[]{:S(2)}) copy-start(bf16[128,128]{1,0:T(8,128)(2,1)} %param.17) | copy-start | bytes 98308
  132.4 1.9 %copy-start.2 = (f32[2048,128]{1,0:T(8,128)S(1)}, f32[2048,128]{1,0:T(8,128)}, u32[]{:S(2)}) copy-start(f32[2048,128]{1,0:T(8,128)} %fusion.11) | copy-start | bytes 3145732
  134.3 1.2 copy-start.6
Sparse Core Ops, SparseCore 0:
  54.6 54.9 all-gather.1
where the time goes:
time: 145 us
  blocking collectives  76.8 us (53%)
  local copies, waits for them, and re-layouts  21.5 us (15%)
  between operations  13.7 us (9%)
  waiting for transfers between devices  11.9 us (8%)
  other arithmetic  8.91 us (6%)
  matrix products  7.95 us (5%)
  starting transfers between devices  3.69 us (3%)
    all_to_all x1, blocking collectives, body(): lax.all_to_all(lax.all_to_all(right_major, 'row', split_axis=0, concat_ax...  31.4 us
    all_to_all x1, blocking collectives, body(): lax.all_to_all(lax.all_to_all(left_major, 'row', split_axis=0, concat_axi...  18.5 us
    all_to_all x1, blocking collectives, body(): lax.all_to_all(left_major, 'row', split_axis=0, concat_axis=1, tiled=True)  14.7 us
    all_to_all x1, blocking collectives, body(): lax.all_to_all(right_major, 'row', split_axis=0, concat_axis=1, tiled=True)  12.2 us
    unnamed x30, local copies, waits for them, and re-layouts  8.68 us
    all_to_all x1, waiting for transfers between devices, body(): lax.all_to_all(mixed, 'row', split_axis=1, concat_axis=0, tiled=True)  8.32 us
    all_to_all x1, starting transfers between devices, body(): lax.all_to_all(mixed, 'row', split_axis=1, concat_axis=0, tiled=True)  3.69 us
    all_gather x1, waiting for transfers between devices, body(): lax.all_gather(left_spread, 'col', axis=1, tiled=True)  3.59 us
  transfers between devices with their start and end apart: 2, of which 2 were waited for; matrix products, arithmetic and copies ran while one was open for 6% of the time, Pallas kernels for 0%

commit v1 on v0

--- a/solution.py
+++ b/solution.py
@@ -2,6 +2,18 @@
 import jax.numpy as jnp
 from jax import lax
 from jax.sharding import PartitionSpec as P
+
+
+def doubled_up(array, axis, dim):
+    ways, here = (lax.axis_size(axis), lax.axis_index(axis))
+    grown, reach = (array, 1)
+    while reach < ways:
+        theirs = lax.ppermute(grown, axis, [(d, d ^ reach) for d in range(ways)])
+        mine_first = jnp.concatenate([grown, theirs], axis=dim)
+        theirs_first = jnp.concatenate([theirs, grown], axis=dim)
+        grown = jnp.where(here & reach == 0, mine_first, theirs_first)
+        reach = 2 * reach
+    return grown
 
 
 def layer_norm(values):
@@ -51,7 +63,7 @@
     )
     mixed = jnp.einsum(
         "cik,cjk->cij",
-        lax.all_gather(left_spread, "col", axis=1, tiled=True),
+        doubled_up(left_spread, "col", 1),
         right_spread,
         preferred_element_type=jnp.float32,
     ).astype(jnp.bfloat16)

time: 145 us -> 150 us (1.034)
  waiting for transfers between devices: 11.9 us -> 62.6 us
  blocking collectives: 76.8 us -> 33.2 us
  between operations: 13.7 us -> 0.39 us
  starting transfers between devices: 3.69 us -> 12.2 us
    all_to_all x0 -> x2, waiting for transfers between devices: none -> 50 us  [the longest x1 47.4 us: body(): lax.all_to_all(lax.all_to_all(right_major, 'row', split_axis=0, concat_ax...]
    all_to_all x2 -> x0, blocking collectives: 43.5 us -> none  [the longest x1 31.4 us: body(): lax.all_to_all(lax.all_to_all(right_major, 'row', split_axis=0, concat_ax...]
    all_to_all x0 -> x2, starting transfers between devices: none -> 7.15 us  [the longest x1 3.67 us: body(): lax.all_to_all(right_major, 'row', split_axis=0, concat_axis=1, tiled=True)]
    ppermute x0 -> x2, waiting for transfers between devices: none -> 4.57 us  [doubled_up(): theirs = lax.ppermute(grown, axis, [(d, d ^ reach) for d in range(ways)])]
    all_gather x1 -> x0, waiting for transfers between devices: 3.59 us -> none  [body(): lax.all_gather(left_spread, 'col', axis=1, tiled=True)]
  transfers between devices with their start and end apart: 2 -> 5, of which waited for: 2 -> 4; matrix products, arithmetic and copies ran while one was open for 6% -> 7% of each run, Pallas kernels for 0% -> 0%
where the time goes in v1:
time: 150 us; the launch traced here: 149 us
  waiting for transfers between devices  62.6 us (42%)
  blocking collectives  33.2 us (22%)
  local copies, waits for them, and re-layouts  22 us (15%)
  starting transfers between devices  12.2 us (8%)
  other arithmetic  10.2 us (7%)
  matrix products  8.62 us (6%)
    all_to_all x1, waiting for transfers between devices, body(): lax.all_to_all(lax.all_to_all(right_major, 'row', split_axis=0, concat_ax...  47.4 us
    all_to_all x1, blocking collectives, body(): lax.all_to_all(lax.all_to_all(left_major, 'row', split_axis=0, concat_axi...  18.5 us
    all_to_all x1, blocking collectives, body(): lax.all_to_all(left_major, 'row', split_axis=0, concat_axis=1, tiled=True)  14.7 us
    unnamed x30, local copies, waits for them, and re-layouts  9.92 us
    all_to_all x1, waiting for transfers between devices, body(): lax.all_to_all(mixed, 'row', split_axis=1, concat_axis=0, tiled=True)  8.04 us
    ppermute x2, waiting for transfers between devices, doubled_up(): theirs = lax.ppermute(grown, axis, [(d, d ^ reach) for d in range(ways)])  4.57 us
    all_to_all x1, starting transfers between devices, body(): lax.all_to_all(mixed, 'row', split_axis=1, concat_axis=0, tiled=True)  3.71 us
    all_to_all x1, starting transfers between devices, body(): lax.all_to_all(right_major, 'row', split_axis=0, concat_axis=1, tiled=True)  3.67 us
  transfers between devices with their start and end apart: 5, of which 4 were waited for; matrix products, arithmetic and copies ran while one was open for 7% of the time, Pallas kernels for 0%

profile of v1, /device:TPU:0, one launch (start us, length us, event | category | flops | bytes accessed | tf_op | source)
XLA Modules:
  0.0 149.2 jit_solution(4402716232668607041)
XLA Ops:
  0.0 1.4 convert_reduce_fusion
  1.4 1.7 %multiply_reduce_fusion.2 = f32[32,64]{1,0:T(8,128)S(1)} fusion(bf16[32,64,128]{2,1,0:T(8,128)(2,1)} %param.10, f32[32,64]{1,0:T(8,128)S(1)} %broadcast_multiply_fusion.2), kind=kLoop, calls=%fused_computation.45 | loop fusion | flops 1046528 | bytes 540672 | tf_op jit(solution)/shard_map/reduce_sum | solution.py:21
  4.3 1.6 %fusion.26 = bf16[2048,128]{1,0:T(8,128)(2,1)S(1)} fusion(bf16[32,64,128]{2,1,0:T(8,128)(2,1)} %param.10, f32[2048]{0:T(1024)S(1)} %rsqrt.31, f32[2048]{0:T(1024)S(1)} %div.32), kind=kLoop, calls=%fused_computation.42 | loop fusion | flops 1048576 | bytes 1064960 | tf_op jit(solution)/shard_map/convert_element_type | solution.py:34
  7.1 1.6 %copy.32 = bf16[32,64,128]{1,0,2:T(8,128)(2,1)S(1)} copy(bf16[32,64,128]{2,1,0:T(8,128)(2,1)S(1)} %bitcast.88) | data formatting | bytes 1048576 | tf_op jit(solution)/shard_map/reshape | solution.py:46
  9.4 14.7 %all_to_all.81 = bf16[8,2,16384]{2,1,0:T(2,128)(2,1)S(1)} all-to-all(bf16[8,2,16384]{2,1,0:T(2,128)(2,1)S(1)} %reshape.123), channel_id=1, replica_groups=mesh['row'=8,'col'=4] {'row'}, dimensions={0} | all-to-all | bytes 1048576 | tf_op jit(solution)/shard_map/all_to_all | solution.py:50
  26.4 18.5 %all_to_all.82 = bf16[4,2,32768]{2,1,0:T(2,128)(2,1)S(1)} all-to-all(bf16[4,2,32768]{2,1,0:T(2,128)(2,1)S(1)} %reshape.125), channel_id=1, replica_groups=mesh['row'=8,'col'=4] {'col'}, dimensions={0} | all-to-all | bytes 1048576 | tf_op jit(solution)/shard_map/all_to_all | solution.py:49
  48.3 1.6 %copy.37 = bf16[32,64,128]{1,0,2:T(8,128)(2,1)S(1)} copy(bf16[32,64,128]{2,1,0:T(8,128)(2,1)S(1)} %bitcast.87) | data formatting | bytes 1048576 | tf_op jit(solution)/shard_map/reshape | solution.py:47
  49.9 1.5 %reshape.119 = bf16[8,2,16384]{2,1,0:T(2,128)(2,1)} reshape(bf16[128,32,64]{2,1,0:T(8,128)(2,1)S(1)} %bitcast.74) | data formatting | bytes 1048576
  51.4 3.7 %all-to-all-start.2 = ((bf16[8,2,16384]{2,1,0:T(2,128)(2,1)}), bf16[8,2,16384]{2,1,0:T(2,128)(2,1)S(1)}, u32[]{:S(2)}, u32[]{:S(2)}) async-start(bf16[8,2,16384]{2,1,0:T(2,128)(2,1)} %reshape.119), calls=%async_computation.2 | async-start | bytes 1048576 | tf_op jit(solution)/shard_map/all_to_all | solution.py:57
  55.1 4.6 %collective-permute-done = bf16[16,64,256]{2,1,0:T(8,128)(2,1)S(1)} collective-permute-done((bf16[16,64,256]{2,1,0:T(8,128)(2,1)S(1)}, bf16[16,64,256]{2,1,0:T(8,128)(2,1)S(1)}, u32[]{:S(2)}, u32[]{:S(2)}) %collective-permute-start) | collective-permute-done | bytes 524320 | tf_op jit(solution)/shard_map/ppermute | solution.py:11
  59.7 1.3 maximum_select_fusion.4
  61.0 1.0 collective-permute-start.1
  62.0 2.6 %all-to-all-done.2 = bf16[8,2,16384]{2,1,0:T(2,128)(2,1)S(1)} async-done(((bf16[8,2,16384]{2,1,0:T(2,128)(2,1)}), bf16[8,2,16384]{2,1,0:T(2,128)(2,1)S(1)}, u32[]{:S(2)}, u32[]{:S(2)}) %all-to-all-start.2) | async-done | bytes 524320 | tf_op jit(solution)/shard_map/all_to_all | solution.py:57
  66.1 1.6 %reshape.121 = bf16[4,2,32768]{2,1,0:T(2,128)(2,1)} reshape(bf16[256,16,64]{2,1,0:T(8,128)(2,1)S(1)} %bitcast.83) | data formatting | bytes 1048576
  67.6 3.5 %all-to-all-start.3 = ((bf16[4,2,32768]{2,1,0:T(2,128)(2,1)}), bf16[4,2,32768]{2,1,0:T(2,128)(2,1)S(1)}, u32[]{:S(2)}, u32[]{:S(2)}) async-start(bf16[4,2,32768]{2,1,0:T(2,128)(2,1)} %reshape.121), calls=%async_computation.3 | async-start | bytes 1048576 | tf_op jit(solution)/shard_map/all_to_all | solution.py:56
  71.1 47.4 %all-to-all-done.3 = bf16[4,2,32768]{2,1,0:T(2,128)(2,1)S(1)} async-done(((bf16[4,2,32768]{2,1,0:T(2,128)(2,1)}), bf16[4,2,32768]{2,1,0:T(2,128)(2,1)S(1)}, u32[]{:S(2)}, u32[]{:S(2)}) %all-to-all-start.3) | async-done | bytes 524320 | tf_op jit(solution)/shard_map/all_to_all | solution.py:56
  120.8 3.0 %fusion.22 = bf16[16,256,64]{1,2,0:T(8,128)(2,1)S(1)} fusion(bf16[16,64,256]{2,1,0:T(8,128)(2,1)S(1)} %all_to_all.74, bf16[16,128,256]{2,1,0:T(8,128)(2,1)} %collective-permute-done.1, bf16[16,128,256]{2,1,0:T(8,128)(2,1)} %maximum_select_fusion.4, pred[]{:T(512)S(6)} %eq.6), kind=kOutput, calls=%fused_computation.33 | convolution fusion | flops 143917056 | bytes 3145729 | tf_op jit(solution)/shard_map/cik,cjk->cij/dot_general | solution.py:64
  124.8 1.5 %reshape.127 = bf16[8,2,16384]{2,1,0:T(2,128)(2,1)} reshape(bf16[256,16,64]{2,1,0:T(8,128)(2,1)S(1)} %bitcast.75) | data formatting | bytes 1048576
  126.3 3.7 %all-to-all-start.4 = ((bf16[8,2,16384]{2,1,0:T(2,128)(2,1)}), bf16[8,2,16384]{2,1,0:T(2,128)(2,1)S(1)}, u32[]{:S(2)}, u32[]{:S(2)}) async-start(bf16[8,2,16384]{2,1,0:T(2,128)(2,1)} %reshape.127), calls=%async_computation.4 | async-start | bytes 1048576 | tf_op jit(solution)/shard_map/all_to_all | solution.py:70
  130.0 1.4 fusion.11
  131.4 8.0 %all-to-all-done.4 = bf16[8,2,16384]{2,1,0:T(2,128)(2,1)S(1)} async-done(((bf16[8,2,16384]{2,1,0:T(2,128)(2,1)}), bf16[8,2,16384]{2,1,0:T(2,128)(2,1)S(1)}, u32[]{:S(2)}, u32[]{:S(2)}) %all-to-all-start.4) | async-done | bytes 524320 | tf_op jit(solution)/shard_map/all_to_all | solution.py:70
  141.6 2.3 %copy.45 = f32[32,64,128]{2,1,0:T(8,128)} copy(f32[32,64,128]{1,0,2:T(8,128)S(1)} %bitcast.70) | data formatting | bytes 2097152 | tf_op jit(solution)/shard_map/convert_element_type | solution.py:71
  144.0 1.9 %fusion.24 = bf16[2048,128]{1,0:T(8,128)(2,1)S(1)} fusion(f32[32,64,128]{2,1,0:T(8,128)} %copy.45, f32[2048]{0:T(1024)S(1)} %rsqrt.33, f32[2048]{0:T(1024)S(1)} %div.38), kind=kLoop, calls=%fused_computation.37 | loop fusion | flops 786432 | bytes 1589248 | tf_op jit(solution)/shard_map/convert_element_type | solution.py:72
  147.1 2.1 %fusion.14 = bf16[2048,128]{1,0:T(8,128)(2,1)} fusion(f32[2048,128]{1,0:T(8,128)S(1)} %get-tuple-element.6, bf16[512,128]{1,0:T(8,128)(2,1)S(1)} %copy-done, bf16[128,512]{1,0:T(8,128)(2,1)S(1)} %copy-done.6, f32[2048]{0:T(1024)S(1)} %add_rsqrt_fusion.2, f32[2048]{0:T(1024)S(1)} %broadcast_multiply_fusion.3), kind=kOutput, calls=%fused_computation.22 | convolution fusion | flops 540278784 | bytes 1851392 | tf_op jit(solution)/shard_map/dot_general | solution.py:78
  (64 shorter events, 16.4 us)
Async XLA Ops:
  0.0 147.1 %copy-start = (bf16[512,128]{1,0:T(8,128)(2,1)S(1)}, bf16[512,128]{1,0:T(8,128)(2,1)}, u32[]{:S(2)}) copy-start(bf16[512,128]{1,0:T(8,128)(2,1)} %param.19) | copy-start | bytes 393220
  0.0 5.9 %copy-start.7 = (bf16[128,128]{1,0:T(8,128)(2,1)S(1)}, bf16[128,128]{1,0:T(8,128)(2,1)}, u32[]{:S(2)}) copy-start(bf16[128,128]{1,0:T(8,128)(2,1)} %param.12) | copy-start | bytes 98308
  5.9 0.8 copy-start.3
  45.7 1.8 %copy-start.8 = (bf16[128,128]{1,0:T(8,128)(2,1)S(1)}, bf16[128,128]{1,0:T(8,128)(2,1)}, u32[]{:S(2)}) copy-start(bf16[128,128]{1,0:T(8,128)(2,1)} %param.14) | copy-start | bytes 98308
  47.2 0.8 copy-start.4
  47.2 12.5 %collective-permute-start = (bf16[16,64,256]{2,1,0:T(8,128)(2,1)S(1)}, bf16[16,64,256]{2,1,0:T(8,128)(2,1)S(1)}, u32[]{:S(2)}, u32[]{:S(2)}) collective-permute-start(bf16[16,64,256]{2,1,0:T(8,128)(2,1)S(1)} %all_to_all.66), channel_id=1, source_target_pairs={{0,1},{1,0},{2,3},{3,2},{4,5},{5,4},{6,7},{7,6},{8,9},{9,8},{10,11... | collective-permute-start | bytes 1572872 | tf_op jit(solution)/shard_map/ppermute | solution.py:11
  51.4 13.2 %all-to-all-start.2 = ((bf16[8,2,16384]{2,1,0:T(2,128)(2,1)}), bf16[8,2,16384]{2,1,0:T(2,128)(2,1)S(1)}, u32[]{:S(2)}, u32[]{:S(2)}) async-start(bf16[8,2,16384]{2,1,0:T(2,128)(2,1)} %reshape.119), calls=%async_computation.2 | async-start | bytes 1048576 | tf_op jit(solution)/shard_map/all_to_all | solution.py:57
  61.0 59.8 %collective-permute-start.1 = (bf16[16,128,256]{2,1,0:T(8,128)(2,1)}, bf16[16,128,256]{2,1,0:T(8,128)(2,1)}, u32[]{:S(2)}, u32[]{:S(2)}) collective-permute-start(bf16[16,128,256]{2,1,0:T(8,128)(2,1)} %maximum_select_fusion.4), channel_id=1, source_target_pairs={{0,2},{1,3},{2,0},{3,1},{4,6},{5,7},{6,4},{7,5},{8,10},{9,11},{10,... | collective-permute-start | bytes 3145736 | tf_op jit(solution)/shard_map/ppermute | solution.py:11
  67.6 50.9 %all-to-all-start.3 = ((bf16[4,2,32768]{2,1,0:T(2,128)(2,1)}), bf16[4,2,32768]{2,1,0:T(2,128)(2,1)S(1)}, u32[]{:S(2)}, u32[]{:S(2)}) async-start(bf16[4,2,32768]{2,1,0:T(2,128)(2,1)} %reshape.121), calls=%async_computation.3 | async-start | bytes 1048576 | tf_op jit(solution)/shard_map/all_to_all | solution.py:56
  123.8 6.2 %copy-start.9 = (bf16[128,128]{1,0:T(8,128)(2,1)S(1)}, bf16[128,128]{1,0:T(8,128)(2,1)}, u32[]{:S(2)}) copy-start(bf16[128,128]{1,0:T(8,128)(2,1)} %param.16) | copy-start | bytes 98308
  126.3 13.2 %all-to-all-start.4 = ((bf16[8,2,16384]{2,1,0:T(2,128)(2,1)}), bf16[8,2,16384]{2,1,0:T(2,128)(2,1)S(1)}, u32[]{:S(2)}, u32[]{:S(2)}) async-start(bf16[8,2,16384]{2,1,0:T(2,128)(2,1)} %reshape.127), calls=%async_computation.4 | async-start | bytes 1048576 | tf_op jit(solution)/shard_map/all_to_all | solution.py:70
  141.6 4.3 %copy-start.1 = (bf16[32,64,128]{2,1,0:T(8,128)(2,1)S(1)}, bf16[32,64,128]{2,1,0:T(8,128)(2,1)}, u32[]{:S(2)}) copy-start(bf16[32,64,128]{2,1,0:T(8,128)(2,1)} %param.10) | copy-start | bytes 1572868
  141.6 4.3 %copy-start.5 = (bf16[128,128]{1,0:T(8,128)(2,1)S(1)}, bf16[128,128]{1,0:T(8,128)(2,1)}, u32[]{:S(2)}) copy-start(bf16[128,128]{1,0:T(8,128)(2,1)} %param.17) | copy-start | bytes 98308
  144.0 1.9 %copy-start.2 = (f32[2048,128]{1,0:T(8,128)S(1)}, f32[2048,128]{1,0:T(8,128)}, u32[]{:S(2)}) copy-start(f32[2048,128]{1,0:T(8,128)} %fusion.11) | copy-start | bytes 3145732
  145.9 1.2 copy-start.6
